TPU v7x, 256 devices: a whole 4x4x8 slice. The times are simulated.
256 devices in a mesh: batch: 16 (over x_hi, z), dom: 16 (over x_lo, y, core).
Axes of the slice: x: 4 (x_hi: 2, x_lo: 2; x = x_hi * 2 + x_lo), y: 4, z: 8, core: 2. Of those that a mesh axis runs over, the one named last changes fastest.
Arguments:
- inputs: bfloat16 [32, 64, 68, 256], P('batch', 'dom'), may hold values from -70 to 70
- saved_q: bfloat16 [32, 64, 68, 256], P('batch', 'dom'), may hold values from -6.5 to 6.5
- saved_k: bfloat16 [32, 64, 68, 256], P('batch', 'dom'), may hold values from -6.5 to 6.5
- saved_v: bfloat16 [32, 64, 68, 256], P('batch', 'dom'), may hold values from -6 to 6
- attended: bfloat16 [32, 64, 68, 256], P('batch', 'dom'), may hold values from -6 to 6
- out_cot: bfloat16 [32, 64, 68, 256], P('batch', 'dom'), may hold values from -6 to 6
- conv_weight: bfloat16 [9, 256, 256], replicated, may hold values from -0.125 to 0.125
- qkv_weight: bfloat16 [256, 768], replicated, may hold values from -0.375 to 0.375
- out_weight: bfloat16 [256, 256], replicated, may hold values from -0.375 to 0.375
- norm_gain: float32 [256], replicated, may hold values from 0.5 to 1.5
- norm_shift: float32 [256], replicated, may hold values from -2.5 to 2.5
Outputs:
- input_grad: bfloat16 [32, 64, 68, 256], P('batch', 'dom')
- conv_grad: float32 [9, 256, 256], replicated
- qkv_grad: float32 [256, 768], replicated
- out_grad: float32 [256, 256], replicated
- gain_grad: float32 [256], replicated
- shift_grad: float32 [256], replicated
All inputs are finite; a program needn't handle non-finite values.
Results may differ from a plain program's by a relative error of at most 0.011.
Values may be sent and summed in bfloat16 or wider, within the bound.
No kernel may reach another device: no remote copies, remote signals or barrier semaphores. Data moves between devices by JAX's collectives and lax.ppermute only.
A program may use at most 128 MiB of HBM per device.

v0:
```python
import jax
import jax.numpy as jnp
from jax import lax
from jax.sharding import PartitionSpec as P

HEADS = 1
GROUPS = 32
EPSILON = 1e-05


def with_halo(cells, sides, width):
    for axis, dim in sides:
        count = lax.axis_size(axis)
        ends = count - 1
        head = lax.slice_in_dim(cells, 0, width, axis=dim)
        tail = lax.slice_in_dim(cells, cells.shape[dim] - width, cells.shape[dim], axis=dim)
        cells = jnp.concatenate(
            [
                lax.ppermute(tail, axis, [(i, (i + 1) % count) for i in range(ends)]),
                cells,
                lax.ppermute(head, axis, [((i + 1) % count, i) for i in range(ends)]),
            ],
            axis=dim,
        )
    return cells


def per_channel(values, group_width):
    return jnp.repeat(values, group_width, axis=-1)[:, None, None, :]


def body(
    inputs,
    saved_q,
    saved_k,
    saved_v,
    attended,
    out_cot,
    conv_weight,
    qkv_weight,
    out_weight,
    norm_gain,
    norm_shift,
):
    samples, row_count, col_count, chan_count = inputs.shape
    tok_count = row_count * col_count
    group_width = chan_count // GROUPS
    head_width = chan_count // HEADS
    score_scale = head_width ** (-0.5)
    count = row_count * col_count * group_width * lax.axis_size("dom")
    f32 = jnp.float32
    bf16 = jnp.bfloat16
    input_wide = inputs.astype(f32)
    grouped = input_wide.reshape(samples, row_count, col_count, GROUPS, group_width)
    group_sums = lax.psum((grouped.sum((1, 2, 4)), (grouped * grouped).sum((1, 2, 4))), "dom")
    group_mean = group_sums[0] / count
    group_var = group_sums[1] / count - group_mean * group_mean
    inv_std = lax.rsqrt(group_var + EPSILON)
    normed = (input_wide - per_channel(group_mean, group_width)) * per_channel(inv_std, group_width)
    pre_act = normed * norm_gain + norm_shift
    sigmoid_pre = jax.nn.sigmoid(pre_act)
    activated = (pre_act * sigmoid_pre).astype(bf16)
    padded = with_halo(activated, (("dom", 1),), 1)
    padded = jnp.pad(padded, ((0, 0), (0, 0), (1, 1), (0, 0)))

    def shifted(source, row_start, col_start):
        return source[
            :, row_start : row_start + row_count, col_start : col_start + col_count, :
        ].reshape(-1, chan_count)

    conv_sum = input_wide.reshape(-1, chan_count)
    for tap_index in range(9):
        row_off = tap_index // 3 - 1
        col_off = tap_index % 3 - 1
        conv_sum = conv_sum + jnp.dot(
            shifted(padded, 1 + row_off, 1 + col_off),
            conv_weight[tap_index],
            preferred_element_type=f32,
        )
    residual = conv_sum.astype(bf16)
    out_flat = out_cot.reshape(-1, chan_count)
    attended_flat = attended.reshape(-1, chan_count)
    out_grad = jnp.einsum("nc,nd->cd", attended_flat, out_flat, preferred_element_type=f32)
    d_attended = jnp.einsum("nd,cd->nc", out_flat, out_weight, preferred_element_type=f32).astype(
        bf16
    )

    def split_heads(values):
        return values.reshape(samples, -1, HEADS, head_width)

    def scores(left, right):
        return jnp.einsum("sqhd,skhd->shqk", left, right, preferred_element_type=f32) * score_scale

    q_rows = saved_q.reshape(samples, tok_count, chan_count)
    k_rows = saved_k.reshape(samples, tok_count, chan_count)
    v_rows = saved_v.reshape(samples, tok_count, chan_count)
    do_rows = d_attended.reshape(samples, tok_count, chan_count)
    q_heads = split_heads(q_rows)
    k_heads = split_heads(k_rows)
    v_heads = split_heads(v_rows)
    do_heads = split_heads(do_rows)
    row_dot = jnp.einsum(
        "sqhd,sqhd->sqh",
        split_heads(attended.reshape(samples, tok_count, chan_count)),
        do_heads,
        preferred_element_type=f32,
    )
    row_dot_t = row_dot.transpose(0, 2, 1)

    def grad_terms(query_heads, dout_heads, key_heads, value_heads, log_norm_t, dot_t):
        softmax_p = jnp.exp(scores(query_heads, key_heads) - log_norm_t[..., None])
        d_probs = jnp.einsum("sqhd,skhd->shqk", dout_heads, value_heads, preferred_element_type=f32)
        d_scores = (softmax_p * (d_probs - dot_t[..., None])).astype(bf16)
        return (softmax_p.astype(bf16), d_scores)

    row_max = jnp.full((samples, HEADS, tok_count), -jnp.inf, f32)
    row_total = jnp.zeros((samples, HEADS, tok_count), f32)
    logits = scores(q_heads, split_heads(lax.all_gather(k_rows, "dom", axis=1, tiled=True)))
    new_max = logits.max(-1)
    row_total = row_total * jnp.exp(row_max - new_max) + jnp.exp(logits - new_max[..., None]).sum(
        -1
    )
    row_max, row_total = (new_max, row_total)
    log_norm = row_max + jnp.log(row_total)
    shard_piece = (
        lax.all_gather(k_rows, "dom", axis=1, tiled=True),
        lax.all_gather(v_rows, "dom", axis=1, tiled=True),
    )
    key_heads = split_heads(shard_piece[0])
    value_heads = split_heads(shard_piece[1])
    p_half, d_scores = grad_terms(q_heads, do_heads, key_heads, value_heads, log_norm, row_dot_t)
    q_accum = jnp.einsum("shqk,skhd->sqhd", d_scores, key_heads, preferred_element_type=f32)
    stats_all = (
        lax.all_gather(log_norm.transpose(0, 2, 1), "dom", axis=1, tiled=True),
        lax.all_gather(row_dot, "dom", axis=1, tiled=True),
    )
    shard_piece = (
        lax.all_gather(q_rows, "dom", axis=1, tiled=True),
        lax.all_gather(do_rows, "dom", axis=1, tiled=True),
    )
    query_heads = split_heads(shard_piece[0])
    dout_heads = split_heads(shard_piece[1])
    norm_piece = stats_all[0].transpose(0, 2, 1)
    dot_piece = stats_all[1].transpose(0, 2, 1)
    p_half, d_scores = grad_terms(query_heads, dout_heads, k_heads, v_heads, norm_piece, dot_piece)
    k_accum = jnp.einsum("shqk,sqhd->skhd", d_scores, query_heads, preferred_element_type=f32)
    v_accum = jnp.einsum("shqk,sqhd->skhd", p_half, dout_heads, preferred_element_type=f32)
    k_accum, v_accum = (k_accum, v_accum)
    k_grad = (k_accum * score_scale).astype(bf16).reshape(samples, tok_count, chan_count)
    v_grad = v_accum.astype(bf16).reshape(samples, tok_count, chan_count)
    q_grad = (q_accum * score_scale).astype(bf16).reshape(samples, tok_count, chan_count)
    proj_grad = jnp.concatenate([q_grad, k_grad, v_grad], axis=-1).reshape(-1, 3 * chan_count)
    qkv_local = jnp.einsum("nc,nd->cd", residual, proj_grad, preferred_element_type=f32)
    d_residual = (
        out_flat.astype(f32)
        + jnp.einsum("nd,cd->nc", proj_grad, qkv_weight, preferred_element_type=f32)
    ).astype(bf16)
    d_res_map = d_residual.reshape(samples, row_count, col_count, chan_count)
    d_padded = with_halo(d_res_map, (("dom", 1),), 1)
    d_padded = jnp.pad(d_padded, ((0, 0), (0, 0), (1, 1), (0, 0)))
    conv_parts = []
    d_act = jnp.zeros((samples * tok_count, chan_count), f32)
    for tap_index in range(9):
        row_off = tap_index // 3 - 1
        col_off = tap_index % 3 - 1
        conv_parts.append(
            jnp.einsum(
                "nc,nd->cd",
                shifted(padded, 1 + row_off, 1 + col_off),
                d_residual,
                preferred_element_type=f32,
            )
        )
        d_act = d_act + jnp.einsum(
            "nd,cd->nc",
            shifted(d_padded, 1 - row_off, 1 - col_off),
            conv_weight[tap_index],
            preferred_element_type=f32,
        )
    conv_local = jnp.stack(conv_parts)
    d_pre = (
        d_act.reshape(samples, row_count, col_count, chan_count)
        * sigmoid_pre
        * (1.0 + pre_act * (1.0 - sigmoid_pre))
    )
    gain_local = (d_pre * normed).sum((0, 1, 2))
    shift_local = d_pre.sum((0, 1, 2))
    scaled = d_pre * norm_gain
    scaled_groups = scaled.reshape(samples, row_count, col_count, GROUPS, group_width)
    product_groups = (scaled * normed).reshape(samples, row_count, col_count, GROUPS, group_width)
    back_sums = lax.psum((scaled_groups.sum((1, 2, 4)), product_groups.sum((1, 2, 4))), "dom")
    first = back_sums[0] / count
    second = back_sums[1] / count
    input_grad = (
        d_res_map.astype(f32)
        + per_channel(inv_std, group_width)
        * (scaled - per_channel(first, group_width) - normed * per_channel(second, group_width))
    ).astype(bf16)
    out_grad, qkv_grad, conv_grad, gain_grad, shift_grad = lax.psum(
        (out_grad, qkv_local, conv_local, gain_local, shift_local), ("batch", "dom")
    )
    return (input_grad, conv_grad, qkv_grad, out_grad, gain_grad, shift_grad)


def solution(mesh):
    placed = (
        P("batch", "dom", None, None),
        P("batch", "dom", None, None),
        P("batch", "dom", None, None),
        P("batch", "dom", None, None),
        P("batch", "dom", None, None),
        P("batch", "dom", None, None),
        P(),
        P(),
        P(),
        P(),
        P(),
    )
    return jax.shard_map(
        body,
        mesh=mesh,
        in_specs=placed,
        out_specs=(P("batch", "dom", None, None), P(), P(), P(), P(), P()),
        check_vma=False,
    )
```

profile of v0, /device:TPU:2, one launch (start us, length us, event | category | flops | bytes accessed | tf_op | source)
XLA Modules:
  0.0 552.1 jit_solution(14365072272132767426)
XLA Ops:
  15.4 19.1 %all-gather.1 = f32[16,272,2]{1,2,0:T(2,128)S(1)} all-gather(f32[1,272,2]{1,2,0:T(2,128)S(1)} %bitcast.194), channel_id=2, replica_groups=mesh['batch'=16,'dom'=16] {'dom'}, dimensions={0}, use_global_device_ids=true | all-gather | bytes 36992 | tf_op jit(solution)/shard_map/all_gather | solution.py:135
  35.1 27.5 %all-reduce.5 = (f32[2,32]{1,0:T(2,128)S(1)}, f32[2,32]{1,0:T(2,128)S(1)}) all-reduce(f32[2,32]{1,0:T(2,128)S(1)} %reduce_sum.100, f32[2,32]{1,0:T(2,128)S(1)} %reduce_sum.81), channel_id=1, replica_groups=mesh['batch'=16,'dom'=16] {'dom'}, use_global_device_ids=true, to_apply=%region_7.8 | all-reduce | flops 128 | bytes 1024 | tf_op jit(solution)/shard_map/psum | solution.py:55
  63.5 3.8 fusion.91
  68.7 2.2 copy-done.1
  71.8 34.4 %all_gather.22 = f32[2,4352,1]{0,2,1:T(1,128)S(1)} all-gather(f32[2,272,1]{0,2,1:T(1,128)} %copy.68), channel_id=1, replica_groups=mesh['batch'=16,'dom'=16] {'dom'}, dimensions={1}, use_global_device_ids=true | all-gather | bytes 36992 | tf_op jit(solution)/shard_map/all_gather | solution.py:134
  106.9 7.5 %subtract_exponential_fusion = f32[2,4352,272]{1,2,0:T(8,128)} fusion(bf16[2,4352,256]{2,1,0:T(8,128)(2,1)} %all-gather.11.cloned.1.call-done, f32[2,4352]{1,0:T(2,128)S(1)} %copy.69, bf16[2,272,256]{2,0,1:T(2,128)(2,1)S(1)} %bitcast.185), kind=kOutput, calls=%fused_computation.1 | convolution fusion | flops 1216888832 | bytes 14239744 | tf_op jit(solution)/shard_map/sqhd,skhd->shqk/dot_general | solution.py:92
  114.3 29.6 %all-gather.13.cloned.1.call-done = bf16[2,4352,256]{2,1,0:T(8,128)(2,1)} async-done(((bf16[2,272,256]{2,1,0:T(8,128)(2,1)}), bf16[2,4352,256]{2,1,0:T(8,128)(2,1)}) %all-gather.13.cloned.1.call-update) | async-done | bytes 4456464 | tf_op jit(solution)/shard_map/all_gather | solution.py:139
  143.9 6.3 %fusion.13 = bf16[2,256,272]{1,2,0:T(8,128)(2,1)S(1)} fusion(bf16[2,4352,256]{2,1,0:T(8,128)(2,1)} %all-gather.13.cloned.1.call-done, f32[2,4352,272]{1,2,0:T(8,128)} %subtract_exponential_fusion), kind=kOutput, calls=%fused_computation.32 | convolution fusion | flops 1214660608 | bytes 14204928 | tf_op jit(solution)/shard_map/shqk,sqhd->skhd/dot_general | solution.py:147
  150.3 9.0 %fusion.12 = bf16[2,272,256]{2,1,0:T(8,128)(2,1)S(1)} fusion(bf16[2,4352,256]{2,1,0:T(8,128)(2,1)} %all-gather.11.cloned.1.call-done, f32[2,4352,272]{1,2,0:T(8,128)} %subtract_exponential_fusion, bf16[2,4352,256]{2,1,0:T(8,128)(2,1)} %all-gather.13.cloned.1.call-done, f32[2,4352]{1,0:T(2,128)S(1)} %bitcast.189, bf16[2,272,256]{2,0,1:T(2,128)(2,1)S(1)} %bitcast.187), kind=kOutput, calls=%fused_computation.31 | convolution fusion | flops 2431688704 | bytes 18974720 | tf_op jit(solution)/shard_map/shqk,sqhd->skhd/dot_general | solution.py:146
  159.3 26.3 %all-gather.9.cloned.1.call-done = bf16[2,4352,256]{2,0,1:T(2,128)(2,1)} async-done(((bf16[2,272,256]{2,0,1:T(2,128)(2,1)}), bf16[2,4352,256]{2,0,1:T(2,128)(2,1)}) %all-gather.9.cloned.1.call-update) | async-done | bytes 4456464 | tf_op jit(solution)/shard_map/all_gather | solution.py:127
  185.6 10.2 %fusion.18 = bf16[2,272,256]{2,1,0:T(8,128)(2,1)S(1)} fusion(bf16[2,4352,256]{2,1,0:T(8,128)(2,1)} %all-gather.7.cloned.1.call-done, f32[2,272,4352]{2,1,0:T(8,128)} %copy-done.1, bf16[2,272,256]{2,1,0:T(8,128)(2,1)S(1)} %bitcast.183, f32[2,272]{1,0:T(2,128)S(1)} %copy.80, f32[2,272]{1,0:T(2,128)S(1)} %log_add_fusion, ...), kind=kOutput, calls=%fused_computation.36 | convolution fusion | flops 2434056192 | bytes 18944256 | tf_op jit(solution)/shard_map/shqk,skhd->sqhd/dot_general | solution.py:132
  197.0 2.1 collective-permute-start
  199.2 5.8 %collective-permute-start.1 = (bf16[2,1,68,256]{3,2,1,0:T(8,128)(2,1)S(1)}, bf16[2,1,68,256]{3,2,1,0:T(8,128)(2,1)S(1)}, u32[]{:S(2)}, u32[]{:S(2)}) collective-permute-start(bf16[2,1,68,256]{3,2,1,0:T(8,128)(2,1)S(1)} %get-tuple-element.59), channel_id=1, source_target_pairs={{1,0},{2,1},{3,2},{4,3},{5,4},{6,5},{7,6},{8,7},{9,8},{10,9},{11,1... | collective-permute-start | bytes 208904 | tf_op jit(solution)/shard_map/ppermute | solution.py:21
  229.4 5.8 %collective-permute-start.3 = (bf16[2,1,68,256]{3,2,1,0:T(8,128)(2,1)S(1)}, bf16[2,1,68,256]{3,2,1,0:T(8,128)(2,1)S(1)}, u32[]{:S(2)}, u32[]{:S(2)}) collective-permute-start(bf16[2,1,68,256]{3,2,1,0:T(8,128)(2,1)S(1)} %get-tuple-element.55), channel_id=1, source_target_pairs={{1,0},{2,1},{3,2},{4,3},{5,4},{6,5},{7,6},{8,7},{9,8},{10,9},{11,1... | collective-permute-start | bytes 208904 | tf_op jit(solution)/shard_map/ppermute | solution.py:21
  235.2 2.0 convolution_bitcast_fusion
  242.9 2.0 fusion.30
  244.8 2.2 convolution_add_fusion.7
  256.4 2.0 fusion.29
  258.3 2.0 fusion.28
  269.3 3.2 fusion.21
  272.9 29.0 %all-reduce.4 = (f32[2,32]{1,0:T(2,128)S(1)}, f32[2,32]{1,0:T(2,128)S(1)}) all-reduce(f32[2,32]{1,0:T(2,128)S(1)} %reduce_sum.106, f32[2,32]{1,0:T(2,128)S(1)} %reduce_sum.103), channel_id=1, replica_groups=mesh['batch'=16,'dom'=16] {'dom'}, use_global_device_ids=true, to_apply=%region_13.14 | all-reduce | flops 128 | bytes 1024 | tf_op jit(solution)/shard_map/psum | solution.py:191
  303.3 74.3 %all-reduce.2 = (f32[256]{0:T(256)}, f32[256]{0:T(256)}) all-reduce(f32[256]{0:T(256)S(1)} %get-tuple-element.24, f32[256]{0:T(256)S(1)} %get-tuple-element.27), channel_id=1, replica_groups=mesh['batch'=16,'dom'=16] {'batch','dom'}, use_global_device_ids=true, to_apply=%region_18.19 | all-reduce | flops 512 | bytes 4096 | tf_op jit(solution)/shard_map/psum | solution.py:199
  377.7 163.0 %all-reduce.8.cloned.1.call-done = (f32[9,256,256]{2,1,0:T(8,128)}, f32[256,768]{1,0:T(8,128)}, f32[256,256]{1,0:T(8,128)}) async-done(((f32[9,256,256]{2,1,0:T(8,128)}, f32[256,768]{1,0:T(8,128)}, f32[256,256]{1,0:T(8,128)}), (f32[9,256,256]{2,1,0:T(8,128)}, f32[256,768]{1,0:T(8,128)}, f32[256,256]{1,0:T(8,128)})) %all-reduce.8.cloned.1.call-update) | async-done | bytes 3407888 | tf_op jit(solution)/shard_map/psum | solution.py:199
  540.7 3.3 copy.124
  (165 shorter events, 65.1 us)
Async XLA Ops:
  7.2 189.4 %copy-start = (bf16[256,768]{1,0:T(8,128)(2,1)S(1)}, bf16[256,768]{1,0:T(8,128)(2,1)}, u32[]{:S(2)}) copy-start(bf16[256,768]{1,0:T(8,128)(2,1)} %param.18) | copy-start | bytes 1179652
  7.2 4.1 copy-start.19
  7.2 4.2 copy-start.23
  7.2 5.3 copy-start.18
  7.2 56.2 %all-gather.7.cloned.1.call-start = ((), (), s32[]{:S(2)}) async-start(), calls=%async_computation | async-start | bytes 4734976 | tf_op jit(solution)/shard_map/all_gather | solution.py:126
  9.3 97.6 %all-gather.11.cloned.1.call-start = ((), (), s32[]{:S(2)}) async-start(), calls=%async_computation.2 | async-start | bytes 4734976 | tf_op jit(solution)/shard_map/all_gather | solution.py:138
  11.3 132.7 %all-gather.13.cloned.1.call-start = ((), (), s32[]{:S(2)}) async-start(), calls=%async_computation.3 | async-start | bytes 4734976 | tf_op jit(solution)/shard_map/all_gather | solution.py:139
  11.4 23.2 %copy-start.2 = (bf16[2,4,68,256]{3,1,2,0:T(4,128)(2,1)S(1)}, bf16[2,4,68,256]{3,1,2,0:T(4,128)(2,1)}, u32[]{:S(2)}) copy-start(bf16[2,4,68,256]{3,1,2,0:T(4,128)(2,1)} %param.11) | copy-start | bytes 835588
  12.5 173.2 %all-gather.9.cloned.1.call-start = ((), (), s32[]{:S(2)}) async-start(), calls=%async_computation.1 | async-start | bytes 4734976 | tf_op jit(solution)/shard_map/all_gather | solution.py:127
  13.5 527.2 %all-reduce.8.cloned.1.call-start = ((), (), s32[]{:S(2)}) async-start(), calls=%async_computation.4 | async-start | bytes 6815744 | tf_op jit(solution)/shard_map/psum | solution.py:199
  114.3 36.0 %copy-start.8 = (bf16[2,4,68,256]{3,0,2,1:T(2,128)(2,1)S(1)}, bf16[2,4,68,256]{3,0,2,1:T(2,128)(2,1)}, u32[]{:S(2)}) copy-start(bf16[2,4,68,256]{3,0,2,1:T(2,128)(2,1)} %copy.63) | copy-start | bytes 835588
  150.3 45.6 %copy-start.17 = (bf16[2,256,272]{1,2,0:T(8,128)(2,1)}, bf16[2,256,272]{1,2,0:T(8,128)(2,1)S(1)}, u32[]{:S(2)}) copy-start(bf16[2,256,272]{1,2,0:T(8,128)(2,1)S(1)} %fusion.13) | copy-start | bytes 835588
  150.3 35.4 %copy-start.4 = (bf16[544,256]{1,0:T(8,128)(2,1)S(1)}, bf16[544,256]{1,0:T(8,128)(2,1)}, u32[]{:S(2)}) copy-start(bf16[544,256]{1,0:T(8,128)(2,1)} %convolution_convert_fusion) | copy-start | bytes 835588
  159.3 36.5 %copy-start.21 = (bf16[2,272,256]{2,1,0:T(8,128)(2,1)}, bf16[2,272,256]{2,1,0:T(8,128)(2,1)S(1)}, u32[]{:S(2)}) copy-start(bf16[2,272,256]{2,1,0:T(8,128)(2,1)S(1)} %fusion.12) | copy-start | bytes 835588
  197.0 8.3 %collective-permute-start = (bf16[2,1,68,256]{3,2,1,0:T(8,128)(2,1)S(1)}, bf16[2,1,68,256]{3,2,1,0:T(8,128)(2,1)S(1)}, u32[]{:S(2)}, u32[]{:S(2)}) collective-permute-start(bf16[2,1,68,256]{3,2,1,0:T(8,128)(2,1)S(1)} %get-tuple-element.58), channel_id=1, source_target_pairs={{0,1},{1,2},{2,3},{3,4},{4,5},{5,6},{6,7},{7,8},{8,9},{9,10},{10,1... | collective-permute-start | bytes 208904 | tf_op jit(solution)/shard_map/ppermute | solution.py:19
  199.2 7.5 %collective-permute-start.1 = (bf16[2,1,68,256]{3,2,1,0:T(8,128)(2,1)S(1)}, bf16[2,1,68,256]{3,2,1,0:T(8,128)(2,1)S(1)}, u32[]{:S(2)}, u32[]{:S(2)}) collective-permute-start(bf16[2,1,68,256]{3,2,1,0:T(8,128)(2,1)S(1)} %get-tuple-element.59), channel_id=1, source_target_pairs={{1,0},{2,1},{3,2},{4,3},{5,4},{6,5},{7,6},{8,7},{9,8},{10,9},{11,1... | collective-permute-start | bytes 208904 | tf_op jit(solution)/shard_map/ppermute | solution.py:21
  227.5 11.8 %collective-permute-start.2 = (bf16[2,1,68,256]{3,2,1,0:T(8,128)(2,1)S(1)}, bf16[2,1,68,256]{3,2,1,0:T(8,128)(2,1)S(1)}, u32[]{:S(2)}, u32[]{:S(2)}) collective-permute-start(bf16[2,1,68,256]{3,2,1,0:T(8,128)(2,1)S(1)} %get-tuple-element.54), channel_id=1, source_target_pairs={{0,1},{1,2},{2,3},{3,4},{4,5},{5,6},{6,7},{7,8},{8,9},{9,10},{10,1... | collective-permute-start | bytes 208904 | tf_op jit(solution)/shard_map/ppermute | solution.py:19
  229.4 9.9 %collective-permute-start.3 = (bf16[2,1,68,256]{3,2,1,0:T(8,128)(2,1)S(1)}, bf16[2,1,68,256]{3,2,1,0:T(8,128)(2,1)S(1)}, u32[]{:S(2)}, u32[]{:S(2)}) collective-permute-start(bf16[2,1,68,256]{3,2,1,0:T(8,128)(2,1)S(1)} %get-tuple-element.55), channel_id=1, source_target_pairs={{1,0},{2,1},{3,2},{4,3},{5,4},{6,5},{7,6},{8,7},{9,8},{10,9},{11,1... | collective-permute-start | bytes 208904 | tf_op jit(solution)/shard_map/ppermute | solution.py:21
  248.0 4.5 copy-start.7
  255.3 5.0 copy-start.10
  255.3 5.0 copy-start.11
  255.3 6.2 %copy-start.6 = (bf16[544,256]{1,0:T(8,128)(2,1)S(1)}, bf16[544,256]{1,0:T(8,128)(2,1)}, u32[]{:S(2)}) copy-start(bf16[544,256]{1,0:T(8,128)(2,1)} %reshape.277) | copy-start | bytes 835588
  272.5 29.8 %copy-start.9 = (f32[2,4,68,256]{3,2,1,0:T(8,128)S(1)}, f32[2,4,68,256]{3,2,1,0:T(8,128)}, u32[]{:S(2)}) copy-start(f32[2,4,68,256]{3,2,1,0:T(8,128)} %get-tuple-element.39) | copy-start | bytes 1671172
  540.7 4.2 copy-start.22
  (12 other events, 33.9 us)
Sparse Core Ops, SparseCore 0:
  9.8 42.8 all-gather.6
  55.1 46.8 all-gather.10
  104.3 39.5 all-gather.12
  145.6 39.9 all-gather.8
  272.7 267.9 all-reduce.7
where the time goes:
time: 553 us; the launch traced here: 552 us
  waiting for transfers between devices  220 us (40%)
  blocking collectives  184 us (33%)
  matrix products  69.6 us (13%)
  local copies, waits for them, and re-layouts  39.9 us (7%)
  starting transfers between devices  15.8 us (3%)
  between operations  14.4 us (3%)
  other arithmetic  7.61 us (1%)
    psum x1, waiting for transfers between devices, body(): lax.psum((out_grad, qkv_local, conv_local, gain_local, shift_local), ('ba...  163 us
    psum x1, blocking collectives, body(): lax.psum((out_grad, qkv_local, conv_local, gain_local, shift_local), ('ba...  74.3 us
    all_gather x1, blocking collectives, body(): lax.all_gather(log_norm.transpose(0, 2, 1), 'dom', axis=1, tiled=True)  34.4 us
    all_gather x1, waiting for transfers between devices, body(): lax.all_gather(do_rows, 'dom', axis=1, tiled=True)  29.6 us
    psum x1, blocking collectives, body(): lax.psum((scaled_groups.sum((1, 2, 4)), product_groups.sum((1, 2, 4))), '...  29 us
    psum x1, blocking collectives, body(): lax.psum((grouped.sum((1, 2, 4)), (grouped * grouped).sum((1, 2, 4))), 'd...  27.5 us
    all_gather x1, waiting for transfers between devices, body(): lax.all_gather(v_rows, 'dom', axis=1, tiled=True)  26.3 us
    all_gather x1, blocking collectives, body(): lax.all_gather(row_dot, 'dom', axis=1, tiled=True)  19.1 us
  transfers between devices with their start and end apart: 9, of which 4 were waited for; matrix products, arithmetic and copies ran while one was open for 8% of the time, Pallas kernels for 0%

commit v1 on v0

--- a/solution.py
+++ b/solution.py
@@ -6,6 +6,9 @@
 HEADS = 1
 GROUPS = 32
 EPSILON = 1e-05
+_step_on_block = lambda x_in: jnp.concatenate(
+    lax.all_to_all(jnp.stack([x_in for _ in range(lax.axis_size("dom"))]), "dom", 0, 0), 1
+)
 
 
 def with_halo(cells, sides, width):
@@ -122,10 +125,7 @@
     )
     row_max, row_total = (new_max, row_total)
     log_norm = row_max + jnp.log(row_total)
-    shard_piece = (
-        lax.all_gather(k_rows, "dom", axis=1, tiled=True),
-        lax.all_gather(v_rows, "dom", axis=1, tiled=True),
-    )
+    shard_piece = (lax.all_gather(k_rows, "dom", axis=1, tiled=True), _step_on_block(v_rows))
     key_heads = split_heads(shard_piece[0])
     value_heads = split_heads(shard_piece[1])
     p_half, d_scores = grad_terms(q_heads, do_heads, key_heads, value_heads, log_norm, row_dot_t)

time: 553 us -> 583 us (1.054)
  blocking collectives: 184 us -> 260 us
  waiting for transfers between devices: 220 us -> 163 us
  starting transfers between devices: 15.8 us -> 22.5 us
  local copies, waits for them, and re-layouts: 39.9 us -> 45.8 us
    all_gather x1, blocking collectives: 19.1 us -> 87.3 us  [body(): lax.all_gather(row_dot, 'dom', axis=1, tiled=True)]
    all_gather x1, waiting for transfers between devices: 29.6 us -> 0.01 us  [body(): lax.all_gather(do_rows, 'dom', axis=1, tiled=True)]
    all_gather x1 -> x0, waiting for transfers between devices: 26.3 us -> none  [body(): lax.all_gather(v_rows, 'dom', axis=1, tiled=True)]
    all_to_all x0 -> x1, starting transfers between devices: none -> 6.72 us  [lax.all_to_all(jnp.stack([x_in for _ in range(lax.axis_size('dom'))]), 'd...]
    unnamed x64 -> x70, local copies, waits for them, and re-layouts: 12.5 us -> 11.2 us
  transfers between devices with their start and end apart: 9 -> 9, of which waited for: 4 -> 2; matrix products, arithmetic and copies ran while one was open for 8% -> 6% of each run, Pallas kernels for 0% -> 0%
where the time goes in v1:
time: 583 us; the launch traced here: 582 us
  blocking collectives  260 us (45%)
  waiting for transfers between devices  163 us (28%)
  matrix products  69.5 us (12%)
  local copies, waits for them, and re-layouts  45.8 us (8%)
  starting transfers between devices  22.5 us (4%)
  between operations  14.5 us (2%)
  other arithmetic  6.67 us (1%)
    psum x1, waiting for transfers between devices, body(): lax.psum((out_grad, qkv_local, conv_local, gain_local, shift_local), ('ba...  162 us
    all_gather x1, blocking collectives, body(): lax.all_gather(row_dot, 'dom', axis=1, tiled=True)  87.3 us
    psum x1, blocking collectives, body(): lax.psum((out_grad, qkv_local, conv_local, gain_local, shift_local), ('ba...  79 us
    all_gather x1, blocking collectives, body(): lax.all_gather(log_norm.transpose(0, 2, 1), 'dom', axis=1, tiled=True)  35.2 us
    psum x1, blocking collectives, body(): lax.psum((grouped.sum((1, 2, 4)), (grouped * grouped).sum((1, 2, 4))), 'd...  29.7 us
    psum x1, blocking collectives, body(): lax.psum((scaled_groups.sum((1, 2, 4)), product_groups.sum((1, 2, 4))), '...  28.9 us
    reshape x17, local copies, waits for them, and re-layouts, shifted(): return source[:, row_start:row_start + row_count, col_start:col_start + c...  18 us
    dot_general x9, matrix products, body(): jnp.einsum('nc,nd->cd', shifted(padded, 1 + row_off, 1 + col_off), d_resi...  11.9 us
  transfers between devices with their start and end apart: 9, of which 2 were waited for; matrix products, arithmetic and copies ran while one was open for 6% of the time, Pallas kernels for 0%

profile of v1, /device:TPU:2, one launch (start us, length us, event | category | flops | bytes accessed | tf_op | source)
XLA Modules:
  0.0 582.2 jit_solution(14340100272314735308)
XLA Ops:
  12.8 2.5 stack.33
  15.3 6.7 %all-to-all-start = ((bf16[16,2,272,256]{3,2,1,0:T(8,128)(2,1)}), bf16[16,2,272,256]{3,2,1,0:T(8,128)(2,1)}, u32[]{:S(2)}, u32[]{:S(2)}) async-start(bf16[16,2,272,256]{3,2,1,0:T(8,128)(2,1)} %stack.33), calls=%async_computation | async-start | bytes 8912896 | tf_op jit(solution)/shard_map/all_to_all | solution.py:10
  23.0 87.3 %all-gather.1 = f32[16,272,2]{1,2,0:T(2,128)S(1)} all-gather(f32[1,272,2]{1,2,0:T(2,128)S(1)} %bitcast.199), channel_id=2, replica_groups=mesh['batch'=16,'dom'=16] {'dom'}, dimensions={0}, use_global_device_ids=true | all-gather | bytes 36992 | tf_op jit(solution)/shard_map/all_gather | solution.py:135
  110.9 29.7 %all-reduce.5 = (f32[2,32]{1,0:T(2,128)S(1)}, f32[2,32]{1,0:T(2,128)S(1)}) all-reduce(f32[2,32]{1,0:T(2,128)S(1)} %reduce_sum.100, f32[2,32]{1,0:T(2,128)S(1)} %reduce_sum.81), channel_id=1, replica_groups=mesh['batch'=16,'dom'=16] {'dom'}, use_global_device_ids=true, to_apply=%region_7.8 | all-reduce | flops 128 | bytes 1024 | tf_op jit(solution)/shard_map/psum | solution.py:58
  141.4 4.6 copy.67
  146.1 3.8 fusion.82
  151.3 2.2 copy-done.1
  154.4 35.2 %all_gather.18 = f32[2,4352,1]{0,2,1:T(1,128)S(1)} all-gather(f32[2,272,1]{0,2,1:T(1,128)} %copy.71), channel_id=1, replica_groups=mesh['batch'=16,'dom'=16] {'dom'}, dimensions={1}, use_global_device_ids=true | all-gather | bytes 36992 | tf_op jit(solution)/shard_map/all_gather | solution.py:134
  190.2 7.5 %subtract_exponential_fusion = f32[2,4352,272]{1,2,0:T(8,128)} fusion(bf16[2,4352,256]{2,1,0:T(8,128)(2,1)} %all-gather.8.cloned.1.call-done, f32[2,4352]{1,0:T(2,128)S(1)} %copy.72, bf16[2,272,256]{2,0,1:T(2,128)(2,1)S(1)} %bitcast.190), kind=kOutput, calls=%fused_computation.1 | convolution fusion | flops 1216888832 | bytes 14239744 | tf_op jit(solution)/shard_map/sqhd,skhd->shqk/dot_general | solution.py:95
  197.8 6.6 %fusion.7 = bf16[2,256,272]{1,2,0:T(8,128)(2,1)S(1)} fusion(bf16[2,4352,256]{2,1,0:T(8,128)(2,1)} %all-gather.10.cloned.1.call-done, f32[2,4352,272]{1,2,0:T(8,128)} %subtract_exponential_fusion), kind=kOutput, calls=%fused_computation.31 | convolution fusion | flops 1214660608 | bytes 14204928 | tf_op jit(solution)/shard_map/shqk,sqhd->skhd/dot_general | solution.py:147
  204.4 9.0 %fusion.6 = bf16[2,272,256]{2,1,0:T(8,128)(2,1)S(1)} fusion(bf16[2,4352,256]{2,1,0:T(8,128)(2,1)} %all-gather.8.cloned.1.call-done, f32[2,4352,272]{1,2,0:T(8,128)} %subtract_exponential_fusion, bf16[2,4352,256]{2,1,0:T(8,128)(2,1)} %all-gather.10.cloned.1.call-done, f32[2,4352]{1,0:T(2,128)S(1)} %bitcast.194, bf16[2,272,256]{2,0,1:T(2,128)(2,1)S(1)} %bitcast.192), kind=kOutput, calls=%fused_computation.30 | convolution fusion | flops 2431688704 | bytes 18974720 | tf_op jit(solution)/shard_map/shqk,sqhd->skhd/dot_general | solution.py:146
  213.4 9.8 %fusion.5 = bf16[2,272,256]{2,1,0:T(8,128)(2,1)S(1)} fusion(bf16[2,4352,256]{2,1,0:T(8,128)(2,1)} %all-gather.6.cloned.1.call-done, f32[2,272,4352]{2,1,0:T(8,128)} %copy-done.1, bf16[2,272,256]{2,1,0:T(8,128)(2,1)S(1)} %bitcast.188, bf16[2,4352,256]{2,1,0:T(8,128)(2,1)} %bitcast.183, f32[2,272]{1,0:T(2,128)S(1)} %copy.83, f32[2,272]{1,0:T(2,128)S(1)} %log_add_fusion), kind=kOutput, calls=%fused_computation.29 | convolution fusion | flops 2434056192 | bytes 18944256 | tf_op jit(solution)/shard_map/shqk,skhd->sqhd/dot_general | solution.py:132
  223.9 2.2 collective-permute-start
  226.1 5.4 collective-permute-start.1
  254.3 2.1 collective-permute-start.2
  256.5 5.8 collective-permute-start.3
  262.3 2.0 convolution_bitcast_fusion
  269.9 2.0 fusion.21
  271.9 2.2 convolution_add_fusion.7
  296.4 3.2 fusion.12
  300.0 28.9 %all-reduce.4 = (f32[2,32]{1,0:T(2,128)S(1)}, f32[2,32]{1,0:T(2,128)S(1)}) all-reduce(f32[2,32]{1,0:T(2,128)S(1)} %reduce_sum.106, f32[2,32]{1,0:T(2,128)S(1)} %reduce_sum.103), channel_id=1, replica_groups=mesh['batch'=16,'dom'=16] {'dom'}, use_global_device_ids=true, to_apply=%region_13.14 | all-reduce | flops 128 | bytes 1024 | tf_op jit(solution)/shard_map/psum | solution.py:191
  330.3 79.0 %all-reduce.2 = (f32[256]{0:T(256)}, f32[256]{0:T(256)}) all-reduce(f32[256]{0:T(256)S(1)} %get-tuple-element.24, f32[256]{0:T(256)S(1)} %get-tuple-element.27), channel_id=1, replica_groups=mesh['batch'=16,'dom'=16] {'batch','dom'}, use_global_device_ids=true, to_apply=%region_18.19 | all-reduce | flops 512 | bytes 4096 | tf_op jit(solution)/shard_map/psum | solution.py:199
  409.2 161.5 %all-reduce.8.cloned.1.call-done = (f32[9,256,256]{2,1,0:T(8,128)}, f32[256,768]{1,0:T(8,128)}, f32[256,256]{1,0:T(8,128)}) async-done(((f32[9,256,256]{2,1,0:T(8,128)}, f32[256,768]{1,0:T(8,128)}, f32[256,256]{1,0:T(8,128)}), (f32[9,256,256]{2,1,0:T(8,128)}, f32[256,768]{1,0:T(8,128)}, f32[256,256]{1,0:T(8,128)})) %all-reduce.8.cloned.1.call-update) | async-done | bytes 3407888 | tf_op jit(solution)/shard_map/psum | solution.py:199
  570.8 3.3 copy.119
  (173 shorter events, 65.1 us)
Async XLA Ops:
  7.2 216.1 %copy-start = (bf16[256,768]{1,0:T(8,128)(2,1)S(1)}, bf16[256,768]{1,0:T(8,128)(2,1)}, u32[]{:S(2)}) copy-start(bf16[256,768]{1,0:T(8,128)(2,1)} %param.18) | copy-start | bytes 1179652
  7.2 4.3 copy-start.26
  7.2 5.3 copy-start.21
  7.2 138.8 %all-gather.6.cloned.1.call-start = ((), (), s32[]{:S(2)}) async-start(), calls=%async_computation.1 | async-start | bytes 4734976 | tf_op jit(solution)/shard_map/all_gather | solution.py:128
  9.3 180.9 %all-gather.8.cloned.1.call-start = ((), (), s32[]{:S(2)}) async-start(), calls=%async_computation.2 | async-start | bytes 4734976 | tf_op jit(solution)/shard_map/all_gather | solution.py:138
  11.3 186.5 %all-gather.10.cloned.1.call-start = ((), (), s32[]{:S(2)}) async-start(), calls=%async_computation.3 | async-start | bytes 4734976 | tf_op jit(solution)/shard_map/all_gather | solution.py:139
  15.3 6.8 %copy-start.4 = (bf16[544,256]{1,0:T(8,128)(2,1)S(1)}, bf16[544,256]{1,0:T(8,128)(2,1)}, u32[]{:S(2)}) copy-start(bf16[544,256]{1,0:T(8,128)(2,1)} %convolution_convert_fusion) | copy-start | bytes 835588
  15.3 6.8 %copy-start.23 = (bf16[2,4,68,256]{3,1,2,0:T(4,128)(2,1)S(1)}, bf16[2,4,68,256]{3,1,2,0:T(4,128)(2,1)}, u32[]{:S(2)}) copy-start(bf16[2,4,68,256]{3,1,2,0:T(4,128)(2,1)} %param.15) | copy-start | bytes 835588
  15.3 126.1 %all-to-all-start = ((bf16[16,2,272,256]{3,2,1,0:T(8,128)(2,1)}), bf16[16,2,272,256]{3,2,1,0:T(8,128)(2,1)}, u32[]{:S(2)}, u32[]{:S(2)}) async-start(bf16[16,2,272,256]{3,2,1,0:T(8,128)(2,1)} %stack.33), calls=%async_computation | async-start | bytes 8912896 | tf_op jit(solution)/shard_map/all_to_all | solution.py:10
  22.0 88.4 %copy-start.2 = (bf16[2,4,68,256]{3,1,2,0:T(4,128)(2,1)S(1)}, bf16[2,4,68,256]{3,1,2,0:T(4,128)(2,1)}, u32[]{:S(2)}) copy-start(bf16[2,4,68,256]{3,1,2,0:T(4,128)(2,1)} %param.11) | copy-start | bytes 835588
  22.0 548.7 %all-reduce.8.cloned.1.call-start = ((), (), s32[]{:S(2)}) async-start(), calls=%async_computation.4 | async-start | bytes 6815744 | tf_op jit(solution)/shard_map/psum | solution.py:199
  197.8 6.6 %copy-start.9 = (bf16[2,4,68,256]{3,0,2,1:T(2,128)(2,1)S(1)}, bf16[2,4,68,256]{3,0,2,1:T(2,128)(2,1)}, u32[]{:S(2)}) copy-start(bf16[2,4,68,256]{3,0,2,1:T(2,128)(2,1)} %copy-done.8) | copy-start | bytes 835588
  204.4 18.9 %copy-start.20 = (bf16[2,256,272]{1,2,0:T(8,128)(2,1)}, bf16[2,256,272]{1,2,0:T(8,128)(2,1)S(1)}, u32[]{:S(2)}) copy-start(bf16[2,256,272]{1,2,0:T(8,128)(2,1)S(1)} %fusion.7) | copy-start | bytes 835588
  213.4 9.9 %copy-start.24 = (bf16[2,272,256]{2,1,0:T(8,128)(2,1)}, bf16[2,272,256]{2,1,0:T(8,128)(2,1)S(1)}, u32[]{:S(2)}) copy-start(bf16[2,272,256]{2,1,0:T(8,128)(2,1)S(1)} %fusion.6) | copy-start | bytes 835588
  213.4 9.9 %copy-start.14 = (bf16[544,256]{1,0:T(8,128)(2,1)S(1)}, bf16[544,256]{1,0:T(8,128)(2,1)}, u32[]{:S(2)}) copy-start(bf16[544,256]{1,0:T(8,128)(2,1)} %copy-done.13) | copy-start | bytes 835588
  223.9 8.0 %collective-permute-start = (bf16[2,1,68,256]{3,2,1,0:T(8,128)(2,1)S(1)}, bf16[2,1,68,256]{3,2,1,0:T(8,128)(2,1)S(1)}, u32[]{:S(2)}, u32[]{:S(2)}) collective-permute-start(bf16[2,1,68,256]{3,2,1,0:T(8,128)(2,1)S(1)} %get-tuple-element.58), channel_id=1, source_target_pairs={{0,1},{1,2},{2,3},{3,4},{4,5},{5,6},{6,7},{7,8},{8,9},{9,10},{10,1... | collective-permute-start | bytes 208904 | tf_op jit(solution)/shard_map/ppermute | solution.py:22
  226.1 7.4 %collective-permute-start.1 = (bf16[2,1,68,256]{3,2,1,0:T(8,128)(2,1)S(1)}, bf16[2,1,68,256]{3,2,1,0:T(8,128)(2,1)S(1)}, u32[]{:S(2)}, u32[]{:S(2)}) collective-permute-start(bf16[2,1,68,256]{3,2,1,0:T(8,128)(2,1)S(1)} %get-tuple-element.59), channel_id=1, source_target_pairs={{1,0},{2,1},{3,2},{4,3},{5,4},{6,5},{7,6},{8,7},{9,8},{10,9},{11,1... | collective-permute-start | bytes 208904 | tf_op jit(solution)/shard_map/ppermute | solution.py:24
  254.3 12.0 %collective-permute-start.2 = (bf16[2,1,68,256]{3,2,1,0:T(8,128)(2,1)S(1)}, bf16[2,1,68,256]{3,2,1,0:T(8,128)(2,1)S(1)}, u32[]{:S(2)}, u32[]{:S(2)}) collective-permute-start(bf16[2,1,68,256]{3,2,1,0:T(8,128)(2,1)S(1)} %get-tuple-element.54), channel_id=1, source_target_pairs={{0,1},{1,2},{2,3},{3,4},{4,5},{5,6},{6,7},{7,8},{8,9},{9,10},{10,1... | collective-permute-start | bytes 208904 | tf_op jit(solution)/shard_map/ppermute | solution.py:22
  256.5 9.9 %collective-permute-start.3 = (bf16[2,1,68,256]{3,2,1,0:T(8,128)(2,1)S(1)}, bf16[2,1,68,256]{3,2,1,0:T(8,128)(2,1)S(1)}, u32[]{:S(2)}, u32[]{:S(2)}) collective-permute-start(bf16[2,1,68,256]{3,2,1,0:T(8,128)(2,1)S(1)} %get-tuple-element.55), channel_id=1, source_target_pairs={{1,0},{2,1},{3,2},{4,3},{5,4},{6,5},{7,6},{8,7},{9,8},{10,9},{11,1... | collective-permute-start | bytes 208904 | tf_op jit(solution)/shard_map/ppermute | solution.py:24
  275.1 4.5 copy-start.7
  282.4 5.0 copy-start.11
  282.4 5.0 copy-start.12
  282.4 6.1 %copy-start.6 = (bf16[544,256]{1,0:T(8,128)(2,1)S(1)}, bf16[544,256]{1,0:T(8,128)(2,1)}, u32[]{:S(2)}) copy-start(bf16[544,256]{1,0:T(8,128)(2,1)} %reshape.281) | copy-start | bytes 835588
  299.6 29.7 %copy-start.10 = (f32[2,4,68,256]{3,2,1,0:T(8,128)S(1)}, f32[2,4,68,256]{3,2,1,0:T(8,128)}, u32[]{:S(2)}) copy-start(f32[2,4,68,256]{3,2,1,0:T(8,128)} %get-tuple-element.39) | copy-start | bytes 1671172
  (15 other events, 42.1 us)
Sparse Core Ops, SparseCore 0:
  9.8 87.8 all-gather.5
  99.5 45.5 all-gather.7
  147.5 45.7 all-gather.9
  299.7 271.0 all-reduce.7
